TPU v7x, 512 devices: a whole 4x4x16 slice. The times are simulated.
512 devices in a mesh: section: 32 (over z_lo, y, core), seq: 16 (over x, z_hi).
Axes of the slice: x: 4, y: 4, z: 16 (z_hi: 4, z_lo: 4; z = z_hi * 4 + z_lo), core: 2. Of those that a mesh axis runs over, the one named last changes fastest.
Arguments:
- up_activation: bfloat16 [32, 2048, 4096], P('section', 'seq'), as said below
- saved_projections: bfloat16 [32, 2048, 768], P('section', 'seq'), as said below
- up_cotangent: bfloat16 [32, 2048, 4096], P('section', 'seq'), may hold values from -6 to 6
- up_input_weight: bfloat16 [32, 4096, 768], P('section', 'seq'), may hold values from -0.09375 to 0.09375
- up_output_weight: bfloat16 [32, 512, 4096], P('section', None, 'seq'), may hold values from -0.25 to 0.25
- upward_gain: float32 [32, 4096], P('section'), may hold values from 0.5 to 1.5
- accum_input: bfloat16 [32, 4096, 768], P('section', 'seq'), may hold values from -48 to 48
- doc_starts: int32 [32, 2048], P('section', 'seq'), may hold values from 0 to 2047, as said below
Outputs:
- upward_grad: bfloat16 [32, 2048, 4096], P('section', 'seq')
- project_grads: bfloat16 [32, 4096, 768], P('section', 'seq')
Inputs may be any that keep to these rules, and one draw needn't show every extreme that they name: doc_starts[s, t] is the position of the first token of the document holding token t: it is 0 at t = 0, equals t or doc_starts[s, t - 1] elsewhere, and the last token of every micro-batch starts a document. `up_activation`: saved inputs of the upward layers. `saved_projections`: saved queries, keys and values of the upward layers.
All inputs are finite; a program needn't handle non-finite values.
Results may differ from a plain program's by a relative error of at most 0.014.
Values may be sent and summed in bfloat16 or wider, within the bound.
No kernel may reach another device: no remote copies, remote signals or barrier semaphores. Data moves between devices by JAX's collectives and lax.ppermute only.
A program may use at most 64 MiB of HBM per device.

v0:
```python
import jax
import jax.numpy as jnp
from jax import lax
from jax.sharding import PartitionSpec as P

HEAD = 128
GROUP = 4


def shifted(value, axis, steps):
    count = lax.axis_size(axis)
    initial, last = (max(0, -steps), min(count, count - steps))
    return lax.ppermute(value, axis, [(source, source + steps) for source in range(initial, last)])


def from_partner(x, axis, stride):
    return lax.ppermute(x, axis, [(i, i ^ 1 << stride) for i in range(lax.axis_size(axis))])


def contract_last(left, right):
    return lax.dot_general(
        left, right, (((1,), (1,)), ((), ())), preferred_element_type=jnp.float32
    )


def contract_first(left, right):
    return lax.dot_general(
        left, right, (((0,), (0,)), ((), ())), preferred_element_type=jnp.float32
    )


def normalize(values, gain):
    floats = values.astype(jnp.float32)
    inverse = lax.rsqrt(jnp.mean(floats * floats, axis=-1, keepdims=True) + 1e-05)
    unit = floats * inverse
    return (unit, inverse, unit * gain)


def per_device(
    up_activation,
    saved_projections,
    up_cotangent,
    up_input_weight,
    up_output_weight,
    upward_gain,
    accum_input,
    doc_starts,
):
    factor = HEAD ** (-0.5)
    width = GROUP * HEAD
    count = up_activation.shape[1]
    first = lax.axis_index("seq") * count
    saved = saved_projections[0]
    cotangent = up_cotangent[0]
    unit_up, inverse_up, normed_up = normalize(up_activation[0], upward_gain[0])
    hidden = normed_up.astype(jnp.bfloat16)
    key_value = lax.all_gather(saved[:, width:], "seq", axis=0, tiled=True)
    keys = key_value[:, :HEAD]
    values = key_value[:, HEAD:]
    query = saved[:, :width].reshape(count, GROUP, HEAD)
    hidden_cols = lax.all_to_all(hidden, "seq", split_axis=1, concat_axis=0, tiled=True)
    block = cotangent
    attn_grad = contract_last(
        block, lax.all_gather(up_output_weight[0], "seq", axis=1, tiled=True)
    ).astype(jnp.bfloat16)
    positions = first + jnp.arange(count, dtype=jnp.int32)
    key_positions = jnp.arange(keys.shape[0], dtype=jnp.int32)
    starts = doc_starts[0]
    visible = (key_positions[None, :] <= positions[:, None]) & (
        key_positions[None, :] >= starts[:, None]
    )
    scores = jnp.einsum("tgh,jh->tgj", query, keys, preferred_element_type=jnp.float32) * factor
    scores = jnp.where(visible[:, None, :], scores, -1e30)
    top = jnp.max(scores, axis=-1, keepdims=True)
    exps = jnp.where(visible[:, None, :], jnp.exp(scores - top), 0.0)
    probs = exps / jnp.sum(exps, axis=-1, keepdims=True)
    weights = probs.astype(jnp.bfloat16)
    grad_heads = attn_grad.reshape(count, GROUP, HEAD)
    prob_grad = jnp.einsum("tgh,jh->tgj", grad_heads, values, preferred_element_type=jnp.float32)
    inner = jnp.sum(probs * prob_grad, axis=-1, keepdims=True)
    score_grad = (probs * (prob_grad - inner) * factor).astype(jnp.bfloat16)
    query_grad = (
        jnp.einsum("tgj,jh->tgh", score_grad, keys, preferred_element_type=jnp.float32)
        .astype(jnp.bfloat16)
        .reshape(count, width)
    )
    key_part = jnp.einsum("tgj,tgh->jh", score_grad, query, preferred_element_type=jnp.float32)
    value_part = jnp.einsum("tgj,tgh->jh", weights, grad_heads, preferred_element_type=jnp.float32)
    key_total, value_total = (
        lax.psum(key_part.astype(jnp.bfloat16), "seq").astype(jnp.float32),
        lax.psum(value_part.astype(jnp.bfloat16), "seq").astype(jnp.float32),
    )
    kv_grad = jnp.concatenate(
        [key_total.astype(jnp.bfloat16), value_total.astype(jnp.bfloat16)], axis=1
    )
    query_all = lax.all_gather(query_grad, "seq", axis=0, tiled=True)
    grad_all = jnp.concatenate([query_all, kv_grad], axis=1)
    input_term = contract_first(hidden_cols, grad_all).astype(jnp.bfloat16)
    block = contract_last(grad_all, up_input_weight[0])
    hidden_grad = lax.all_to_all(block, "seq", split_axis=0, concat_axis=1, tiled=True)
    scaled = hidden_grad * upward_gain[0]
    input_grad = cotangent.astype(jnp.float32) + inverse_up * (
        scaled - unit_up * jnp.mean(scaled * unit_up, axis=-1, keepdims=True)
    )
    moved_grad = shifted(input_grad.astype(jnp.bfloat16), "section", 1)
    sections = lax.axis_size("section")
    mirror_input = input_term
    for bit in range(sections.bit_length() - 1):
        mirror_input = from_partner(mirror_input, "section", bit)
    project_grads = (accum_input[0].astype(jnp.float32) + mirror_input.astype(jnp.float32)).astype(
        jnp.bfloat16
    )
    return (moved_grad[None], project_grads[None])


def solution(mesh):
    return jax.shard_map(
        per_device,
        mesh=mesh,
        in_specs=(
            P("section", "seq", None),
            P("section", "seq", None),
            P("section", "seq", None),
            P("section", "seq", None),
            P("section", None, "seq"),
            P("section", None),
            P("section", "seq", None),
            P("section", "seq"),
        ),
        out_specs=(P("section", "seq", None), P("section", "seq", None)),
        check_vma=False,
    )
```

profile of v0, /device:TPU:25, one launch (start us, length us, event | category | flops | bytes accessed | tf_op | source)
XLA Modules:
  0.0 827.4 jit_solution(4818707884297721254)
XLA Ops:
  10.7 82.6 %all-gather.5.cloned.1.call-done = bf16[2048,256]{1,0:T(8,128)(2,1)} async-done(((bf16[128,256]{1,0:T(8,128)(2,1)}), bf16[2048,256]{1,0:T(8,128)(2,1)}) %all-gather.5.cloned.1.call-update) | async-done | bytes 1048592 | tf_op jit(solution)/shard_map/all_gather | solution.py:57
  93.3 5.0 fusion.64
  98.4 136.5 %all-gather.9.cloned.1.call-done = bf16[1,512,4096]{2,1,0:T(8,128)(2,1)} async-done(((bf16[1,512,256]{2,1,0:T(8,128)(2,1)}), bf16[1,512,4096]{2,1,0:T(8,128)(2,1)}) %all-gather.9.cloned.1.call-update) | async-done | bytes 4194320 | tf_op jit(solution)/shard_map/all_gather | solution.py:64
  234.9 3.9 fusion.33
  240.5 2.7 fusion.41
  243.2 8.2 fusion.8
  251.5 9.2 %fusion.27 = bf16[128,4,128]{0,2,1:T(8,128)(2,1)} fusion(f32[128,4,2048]{2,0,1:T(8,128)} %fusion.41, bf16[2048,256]{1,0:T(8,128)(2,1)S(1)} %copy-done.6, f32[128,4,2048]{2,0,1:T(8,128)} %get-tuple-element.9, f32[128,4]{0,1:T(4,128)S(1)} %get-tuple-element.8), kind=kOutput, calls=%fused_computation.35 | convolution fusion | flops 275843584 | bytes 17436672 | tf_op jit(solution)/shard_map/tgj,jh->tgh/dot_general | solution.py:83
  260.7 195.4 %all-reduce.3.cloned.1.call-done = (bf16[2048,128]{1,0:T(8,128)(2,1)}, bf16[2048,128]{1,0:T(8,128)(2,1)}) async-done(((bf16[2048,128]{1,0:T(8,128)(2,1)}, bf16[2048,128]{1,0:T(8,128)(2,1)}), (bf16[2048,128]{1,0:T(8,128)(2,1)}, bf16[2048,128]{1,0:T(8,128)(2,1)})) %all-reduce.3.cloned.1.call-update) | async-done | bytes 1048592 | tf_op jit(solution)/shard_map/psum | solution.py:91
  460.2 102.7 %all-gather.7.cloned.1.call-done = bf16[2048,512]{0,1:T(8,128)(2,1)} async-done(((bf16[128,512]{0,1:T(8,128)(2,1)}), bf16[2048,512]{0,1:T(8,128)(2,1)}) %all-gather.7.cloned.1.call-update) | async-done | bytes 2097168 | tf_op jit(solution)/shard_map/all_gather | solution.py:96
  565.0 2.8 copy.31
  567.8 4.2 fusion.43
  572.1 10.1 %all-to-all-start = ((f32[16,128,256]{2,1,0:T(8,128)}), f32[16,128,256]{2,1,0:T(8,128)S(1)}, u32[]{:S(2)}, u32[]{:S(2)}) async-start(f32[16,128,256]{2,1,0:T(8,128)} %fusion.43), calls=%async_computation | async-start | bytes 4194304 | tf_op jit(solution)/shard_map/all_to_all | solution.py:100
  589.8 73.2 %all-to-all-done = f32[16,128,256]{2,1,0:T(8,128)S(1)} async-done(((f32[16,128,256]{2,1,0:T(8,128)}), f32[16,128,256]{2,1,0:T(8,128)S(1)}, u32[]{:S(2)}, u32[]{:S(2)}) %all-to-all-start) | async-done | bytes 2097184 | tf_op jit(solution)/shard_map/all_to_all | solution.py:100
  662.9 3.1 multiply_convert_fusion.1
  666.0 76.9 %all_to_all.32 = bf16[128,16,256]{2,0,1:T(8,128)(2,1)S(1)} all-to-all(bf16[128,16,256]{2,0,1:T(8,128)(2,1)S(1)} %get-tuple-element.6), channel_id=1, replica_groups=mesh['section'=32,'seq'=16] {'seq'}, dimensions={1} | all-to-all | bytes 2097152 | tf_op jit(solution)/shard_map/all_to_all | solution.py:61
  743.9 5.6 collective-permute-start.1
  752.9 2.3 copy.20
  757.8 5.8 collective-permute-done.2
  765.4 2.3 fusion.18
  769.7 6.8 collective-permute-done.3
  776.5 8.9 %collective-permute-start.4 = (bf16[256,768]{1,0:T(8,128)(2,1)S(1)}, bf16[256,768]{1,0:T(8,128)(2,1)S(1)}, u32[]{:S(2)}, u32[]{:S(2)}) collective-permute-start(bf16[256,768]{1,0:T(8,128)(2,1)S(1)} %collective-permute-done.3), channel_id=1, source_target_pairs={{0,128},{16,144},{32,160},{48,176},{64,192},{80,208},{96,224},{112... | collective-permute-start | bytes 1179656 | tf_op jit(solution)/shard_map/ppermute | solution.py:17
  785.4 6.4 collective-permute-done.4
  791.8 11.7 %collective-permute-start.5 = (bf16[256,768]{1,0:T(8,128)(2,1)S(1)}, bf16[256,768]{1,0:T(8,128)(2,1)S(1)}, u32[]{:S(2)}, u32[]{:S(2)}) collective-permute-start(bf16[256,768]{1,0:T(8,128)(2,1)S(1)} %collective-permute-done.4), channel_id=1, source_target_pairs={{0,256},{16,272},{32,288},{48,304},{64,320},{80,336},{96,352},{112... | collective-permute-start | bytes 1179656 | tf_op jit(solution)/shard_map/ppermute | solution.py:17
  804.8 15.2 %collective-permute-done.5 = bf16[256,768]{1,0:T(8,128)(2,1)S(1)} collective-permute-done((bf16[256,768]{1,0:T(8,128)(2,1)S(1)}, bf16[256,768]{1,0:T(8,128)(2,1)S(1)}, u32[]{:S(2)}, u32[]{:S(2)}) %collective-permute-start.5) | collective-permute-done | bytes 393248 | tf_op jit(solution)/shard_map/ppermute | solution.py:17
  (52 shorter events, 32.0 us)
Async XLA Ops:
  7.2 560.7 %copy-start = (bf16[1,256,768]{2,1,0:T(8,128)(2,1)S(1)}, bf16[1,256,768]{2,1,0:T(8,128)(2,1)}, u32[]{:S(2)}) copy-start(bf16[1,256,768]{2,1,0:T(8,128)(2,1)} %param.11) | copy-start | bytes 1179652
  7.2 86.2 %all-gather.5.cloned.1.call-start = ((), (), s32[]{:S(2)}) async-start(), calls=%async_computation.2 | async-start | bytes 1114112 | tf_op jit(solution)/shard_map/all_gather | solution.py:57
  8.8 226.1 %all-gather.9.cloned.1.call-start = ((), (), s32[]{:S(2)}) async-start(), calls=%async_computation.4 | async-start | bytes 4456448 | tf_op jit(solution)/shard_map/all_gather | solution.py:64
  9.5 446.6 %all-reduce.3.cloned.1.call-start = ((), (), s32[]{:S(2)}) async-start(), calls=%async_computation.5 | async-start | bytes 2097152 | tf_op jit(solution)/shard_map/psum | solution.py:91
  10.7 224.2 %copy-start.1 = (bf16[1,128,4096]{2,1,0:T(8,128)(2,1)S(1)}, bf16[1,128,4096]{2,1,0:T(8,128)(2,1)}, u32[]{:S(2)}) copy-start(bf16[1,128,4096]{2,1,0:T(8,128)(2,1)} %param.10) | copy-start | bytes 3145732
  234.9 3.9 copy-start.9
  238.8 1.8 copy-start.6
  240.5 2.7 copy-start.8
  251.4 311.5 %all-gather.7.cloned.1.call-start = ((), (), s32[]{:S(2)}) async-start(), calls=%async_computation.3 | async-start | bytes 2228224 | tf_op jit(solution)/shard_map/all_gather | solution.py:96
  572.1 14.0 %copy-start.7 = (f32[1,4096]{1,0:T(1,128)S(1)}, f32[1,4096]{1,0:T(1,128)}, u32[]{:S(2)}) copy-start(f32[1,4096]{1,0:T(1,128)} %param.13) | copy-start | bytes 49156
  572.1 90.9 %all-to-all-start = ((f32[16,128,256]{2,1,0:T(8,128)}), f32[16,128,256]{2,1,0:T(8,128)S(1)}, u32[]{:S(2)}, u32[]{:S(2)}) async-start(f32[16,128,256]{2,1,0:T(8,128)} %fusion.43), calls=%async_computation | async-start | bytes 4194304 | tf_op jit(solution)/shard_map/all_to_all | solution.py:100
  662.9 80.0 %copy-start.2 = (bf16[2048,512]{0,1:T(8,128)(2,1)S(1)}, bf16[2048,512]{0,1:T(8,128)(2,1)}, u32[]{:S(2)}) copy-start(bf16[2048,512]{0,1:T(8,128)(2,1)} %all-gather.7.cloned.1.call-done) | copy-start | bytes 6291460
  662.9 80.0 %copy-start.3 = (bf16[2048,128]{0,1:T(8,128)(2,1)S(1)}, bf16[2048,128]{0,1:T(8,128)(2,1)}, u32[]{:S(2)}) copy-start(bf16[2048,128]{0,1:T(8,128)(2,1)} %copy.29) | copy-start | bytes 1572868
  662.9 80.0 %copy-start.4 = (bf16[2048,128]{0,1:T(8,128)(2,1)S(1)}, bf16[2048,128]{0,1:T(8,128)(2,1)}, u32[]{:S(2)}) copy-start(bf16[2048,128]{0,1:T(8,128)(2,1)} %copy.30) | copy-start | bytes 1572868
  743.9 7.1 collective-permute-start.1
  751.0 12.5 %collective-permute-start.2 = (bf16[256,768]{1,0:T(8,128)(2,1)}, bf16[256,768]{1,0:T(8,128)(2,1)}, u32[]{:S(2)}, u32[]{:S(2)}) collective-permute-start(bf16[256,768]{1,0:T(8,128)(2,1)} %collective-permute-done.1), channel_id=1, source_target_pairs={{0,32},{16,48},{32,0},{48,16},{64,96},{80,112},{96,64},{112,80},{1... | collective-permute-start | bytes 1179656 | tf_op jit(solution)/shard_map/ppermute | solution.py:17
  757.0 63.1 %copy-start.5 = (bf16[1,256,768]{2,1,0:T(8,128)(2,1)S(1)}, bf16[1,256,768]{2,1,0:T(8,128)(2,1)}, u32[]{:S(2)}) copy-start(bf16[1,256,768]{2,1,0:T(8,128)(2,1)} %param.14) | copy-start | bytes 1179652
  763.5 13.0 %collective-permute-start.3 = (bf16[256,768]{1,0:T(8,128)(2,1)}, bf16[256,768]{1,0:T(8,128)(2,1)S(1)}, u32[]{:S(2)}, u32[]{:S(2)}) collective-permute-start(bf16[256,768]{1,0:T(8,128)(2,1)} %collective-permute-done.2), channel_id=1, source_target_pairs={{0,64},{16,80},{32,96},{48,112},{64,0},{80,16},{96,32},{112,48},{1... | collective-permute-start | bytes 1179656 | tf_op jit(solution)/shard_map/ppermute | solution.py:17
  767.7 35.8 %collective-permute-start = (bf16[128,4096]{0,1:T(8,128)(2,1)S(1)}, bf16[128,4096]{0,1:T(8,128)(2,1)S(1)}, u32[]{:S(2)}, u32[]{:S(2)}) collective-permute-start(bf16[128,4096]{0,1:T(8,128)(2,1)S(1)} %fusion.18), channel_id=1, source_target_pairs={{0,16},{16,32},{32,48},{48,64},{64,80},{80,96},{96,112},{112,128},... | collective-permute-start | bytes 3145736 | tf_op jit(solution)/shard_map/ppermute | solution.py:13
  776.5 15.3 %collective-permute-start.4 = (bf16[256,768]{1,0:T(8,128)(2,1)S(1)}, bf16[256,768]{1,0:T(8,128)(2,1)S(1)}, u32[]{:S(2)}, u32[]{:S(2)}) collective-permute-start(bf16[256,768]{1,0:T(8,128)(2,1)S(1)} %collective-permute-done.3), channel_id=1, source_target_pairs={{0,128},{16,144},{32,160},{48,176},{64,192},{80,208},{96,224},{112... | collective-permute-start | bytes 1179656 | tf_op jit(solution)/shard_map/ppermute | solution.py:17
  791.8 28.2 %collective-permute-start.5 = (bf16[256,768]{1,0:T(8,128)(2,1)S(1)}, bf16[256,768]{1,0:T(8,128)(2,1)S(1)}, u32[]{:S(2)}, u32[]{:S(2)}) collective-permute-start(bf16[256,768]{1,0:T(8,128)(2,1)S(1)} %collective-permute-done.4), channel_id=1, source_target_pairs={{0,256},{16,272},{32,288},{48,304},{64,320},{80,336},{96,352},{112... | collective-permute-start | bytes 1179656 | tf_op jit(solution)/shard_map/ppermute | solution.py:17
Sparse Core Ops, SparseCore 0:
  11.6 81.7 all-gather.4
  96.3 138.4 all-gather.8
  251.5 204.5 all-reduce.2
  460.0 102.9 all-gather.6
where the time goes:
time: 828 us; the launch traced here: 827 us
  waiting for transfers between devices  627 us (76%)
  blocking collectives  76.9 us (9%)
  starting transfers between devices  42.2 us (5%)
  matrix products  36 us (4%)
  local copies, waits for them, and re-layouts  19.1 us (2%)
  between operations  13.9 us (2%)
  other arithmetic  12.5 us (2%)
    psum x1, waiting for transfers between devices, per_device(): lax.psum(value_part.astype(jnp.bfloat16), 'seq').astype(jnp.float32)  195 us
    all_gather x1, waiting for transfers between devices, per_device(): lax.all_gather(up_output_weight[0], 'seq', axis=1, tiled=True)  137 us
    all_gather x1, waiting for transfers between devices, per_device(): query_all = lax.all_gather(query_grad, 'seq', axis=0, tiled=True)  103 us
    all_gather x1, waiting for transfers between devices, per_device(): key_value = lax.all_gather(saved[:, width:], 'seq', axis=0, tiled=True)  82.6 us
    all_to_all x1, blocking collectives, per_device(): lax.all_to_all(hidden, 'seq', split_axis=1, concat_axis=0, tiled=True)  76.9 us
    all_to_all x1, waiting for transfers between devices, per_device(): lax.all_to_all(block, 'seq', split_axis=0, concat_axis=1, tiled=True)  73.2 us
    ppermute x5, waiting for transfers between devices, from_partner(): lax.ppermute(x, axis, [(i, i ^ 1 << stride) for i in range(lax.axis_size(...  35.7 us
    ppermute x5, starting transfers between devices, from_partner(): lax.ppermute(x, axis, [(i, i ^ 1 << stride) for i in range(lax.axis_size(...  30 us
  transfers between devices with their start and end apart: 11, of which 10 were waited for; matrix products, arithmetic and copies ran while one was open for 4% of the time, Pallas kernels for 0%

commit v1 on v0

--- a/solution.py
+++ b/solution.py
@@ -54,7 +54,11 @@
     cotangent = up_cotangent[0]
     unit_up, inverse_up, normed_up = normalize(up_activation[0], upward_gain[0])
     hidden = normed_up.astype(jnp.bfloat16)
-    key_value = lax.all_gather(saved[:, width:], "seq", axis=0, tiled=True)
+    block_2 = saved[:, width:]
+    peers = lax.axis_size("seq")
+    pieces = jnp.stack([block_2 for _ in range(peers)])
+    pieces = lax.all_to_all(pieces, "seq", split_axis=0, concat_axis=0)
+    key_value = jnp.concatenate(pieces, axis=0)
     keys = key_value[:, :HEAD]
     values = key_value[:, HEAD:]
     query = saved[:, :width].reshape(count, GROUP, HEAD)

time: 828 us -> 782 us (0.944)
  waiting for transfers between devices: 627 us -> 566 us
  starting transfers between devices: 42.2 us -> 61.6 us
    all_gather x1 -> x0, waiting for transfers between devices: 82.6 us -> none  [per_device(): key_value = lax.all_gather(saved[:, width:], 'seq', axis=0, tiled=True)]
    all_to_all x0 -> x1, waiting for transfers between devices: none -> 60.4 us  [per_device(): pieces = lax.all_to_all(pieces, 'seq', split_axis=0, concat_axis=0)]
    all_gather x1, waiting for transfers between devices: 137 us -> 97.4 us  [per_device(): lax.all_gather(up_output_weight[0], 'seq', axis=1, tiled=True)]
    all_to_all x0 -> x1, starting transfers between devices: none -> 17.4 us  [per_device(): pieces = lax.all_to_all(pieces, 'seq', split_axis=0, concat_axis=0)]
  transfers between devices with their start and end apart: 11 -> 11, of which waited for: 10 -> 10; matrix products, arithmetic and copies ran while one was open for 4% -> 5% of each run, Pallas kernels for 0% -> 0%
where the time goes in v1:
time: 782 us; the launch traced here: 781 us
  waiting for transfers between devices  566 us (72%)
  blocking collectives  71.6 us (9%)
  starting transfers between devices  61.6 us (8%)
  matrix products  37 us (5%)
  local copies, waits for them, and re-layouts  19.8 us (3%)
  between operations  13.9 us (2%)
  other arithmetic  11.7 us (1%)
    psum x1, waiting for transfers between devices, per_device(): lax.psum(value_part.astype(jnp.bfloat16), 'seq').astype(jnp.float32)  196 us
    all_gather x1, waiting for transfers between devices, per_device(): query_all = lax.all_gather(query_grad, 'seq', axis=0, tiled=True)  103 us
    all_gather x1, waiting for transfers between devices, per_device(): lax.all_gather(up_output_weight[0], 'seq', axis=1, tiled=True)  97.4 us
    all_to_all x1, waiting for transfers between devices, per_device(): lax.all_to_all(block, 'seq', split_axis=0, concat_axis=1, tiled=True)  73.2 us
    all_to_all x1, blocking collectives, per_device(): lax.all_to_all(hidden, 'seq', split_axis=1, concat_axis=0, tiled=True)  71.6 us
    all_to_all x1, waiting for transfers between devices, per_device(): pieces = lax.all_to_all(pieces, 'seq', split_axis=0, concat_axis=0)  60.4 us
    ppermute x5, waiting for transfers between devices, from_partner(): lax.ppermute(x, axis, [(i, i ^ 1 << stride) for i in range(lax.axis_size(...  35.4 us
    ppermute x5, starting transfers between devices, from_partner(): lax.ppermute(x, axis, [(i, i ^ 1 << stride) for i in range(lax.axis_size(...  30.7 us
  transfers between devices with their start and end apart: 11, of which 10 were waited for; matrix products, arithmetic and copies ran while one was open for 5% of the time, Pallas kernels for 0%

profile of v1, /device:TPU:25, one launch (start us, length us, event | category | flops | bytes accessed | tf_op | source)
XLA Modules:
  0.0 781.2 jit_solution(9324347004490086419)
XLA Ops:
  10.2 17.4 %all-to-all-start = ((bf16[16,128,256]{2,1,0:T(8,128)(2,1)}), bf16[16,128,256]{2,1,0:T(8,128)(2,1)S(1)}, u32[]{:S(2)}, u32[]{:S(2)}) async-start(bf16[16,128,256]{2,1,0:T(8,128)(2,1)} %stack.2), calls=%async_computation | async-start | bytes 2097152 | tf_op jit(solution)/shard_map/all_to_all | solution.py:60
  28.2 60.4 %all-to-all-done = bf16[16,128,256]{2,1,0:T(8,128)(2,1)S(1)} async-done(((bf16[16,128,256]{2,1,0:T(8,128)(2,1)}), bf16[16,128,256]{2,1,0:T(8,128)(2,1)S(1)}, u32[]{:S(2)}, u32[]{:S(2)}) %all-to-all-start) | async-done | bytes 1048608 | tf_op jit(solution)/shard_map/all_to_all | solution.py:60
  88.6 4.0 fusion.56
  92.5 97.4 %all-gather.6.cloned.1.call-done = bf16[1,512,4096]{2,1,0:T(8,128)(2,1)} async-done(((bf16[1,512,256]{2,1,0:T(8,128)(2,1)}), bf16[1,512,4096]{2,1,0:T(8,128)(2,1)}) %all-gather.6.cloned.1.call-update) | async-done | bytes 4194320 | tf_op jit(solution)/shard_map/all_gather | solution.py:68
  189.9 3.9 fusion.33
  198.2 10.2 %fusion.8 = bf16[2048,128]{1,0:T(8,128)(2,1)} fusion(bf16[128,4,128]{0,2,1:T(8,128)(2,1)S(1)} %bitcast.99, f32[128,4,2048]{2,0,1:T(8,128)} %fusion.41, f32[128,4,2048]{2,0,1:T(8,128)} %get-tuple-element.9, f32[128,4]{0,1:T(4,128)S(1)} %get-tuple-element.8), kind=kOutput, calls=%fused_computation.13 | convolution fusion | flops 276040192 | bytes 9046016 | tf_op jit(solution)/shard_map/tgj,tgh->jh/dot_general | solution.py:91
  208.5 9.2 %fusion.27 = bf16[128,4,128]{0,2,1:T(8,128)(2,1)} fusion(f32[128,4,2048]{2,0,1:T(8,128)} %fusion.41, bf16[2048,256]{1,0:T(8,128)(2,1)S(1)} %bitcast.93, f32[128,4,2048]{2,0,1:T(8,128)} %get-tuple-element.9, f32[128,4]{0,1:T(4,128)S(1)} %get-tuple-element.8), kind=kOutput, calls=%fused_computation.35 | convolution fusion | flops 275843584 | bytes 17436672 | tf_op jit(solution)/shard_map/tgj,jh->tgh/dot_general | solution.py:87
  217.7 195.6 %all-reduce.3.cloned.1.call-done = (bf16[2048,128]{1,0:T(8,128)(2,1)}, bf16[2048,128]{1,0:T(8,128)(2,1)}) async-done(((bf16[2048,128]{1,0:T(8,128)(2,1)}, bf16[2048,128]{1,0:T(8,128)(2,1)}), (bf16[2048,128]{1,0:T(8,128)(2,1)}, bf16[2048,128]{1,0:T(8,128)(2,1)})) %all-reduce.3.cloned.1.call-update) | async-done | bytes 1048592 | tf_op jit(solution)/shard_map/psum | solution.py:95
  417.5 102.9 %all-gather.4.cloned.1.call-done = bf16[2048,512]{0,1:T(8,128)(2,1)} async-done(((bf16[128,512]{0,1:T(8,128)(2,1)}), bf16[2048,512]{0,1:T(8,128)(2,1)}) %all-gather.4.cloned.1.call-update) | async-done | bytes 2097168 | tf_op jit(solution)/shard_map/all_gather | solution.py:100
  522.4 2.8 copy.31
  525.2 4.3 fusion.43
  529.5 10.1 %all-to-all-start.1 = ((f32[16,128,256]{2,1,0:T(8,128)}), f32[16,128,256]{2,1,0:T(8,128)S(1)}, u32[]{:S(2)}, u32[]{:S(2)}) async-start(f32[16,128,256]{2,1,0:T(8,128)} %fusion.43), calls=%async_computation.1 | async-start | bytes 4194304 | tf_op jit(solution)/shard_map/all_to_all | solution.py:104
  547.2 73.2 %all-to-all-done.1 = f32[16,128,256]{2,1,0:T(8,128)S(1)} async-done(((f32[16,128,256]{2,1,0:T(8,128)}), f32[16,128,256]{2,1,0:T(8,128)S(1)}, u32[]{:S(2)}, u32[]{:S(2)}) %all-to-all-start.1) | async-done | bytes 2097184 | tf_op jit(solution)/shard_map/all_to_all | solution.py:104
  620.3 3.0 multiply_convert_fusion.1
  623.3 71.6 %all_to_all.37 = bf16[128,16,256]{2,0,1:T(8,128)(2,1)S(1)} all-to-all(bf16[128,16,256]{2,0,1:T(8,128)(2,1)S(1)} %get-tuple-element.6), channel_id=1, replica_groups=mesh['section'=32,'seq'=16] {'seq'}, dimensions={1} | all-to-all | bytes 2097152 | tf_op jit(solution)/shard_map/all_to_all | solution.py:65
  696.0 4.2 collective-permute-start.1
  701.7 5.5 collective-permute-start.2
  712.0 4.7 collective-permute-done.2
  716.7 7.0 collective-permute-start.3
  726.0 3.3 collective-permute-start
  732.1 7.1 collective-permute-start.4
  739.2 10.9 %collective-permute-done.4 = bf16[256,768]{1,0:T(8,128)(2,1)S(1)} collective-permute-done((bf16[256,768]{1,0:T(8,128)(2,1)S(1)}, bf16[256,768]{1,0:T(8,128)(2,1)S(1)}, u32[]{:S(2)}, u32[]{:S(2)}) %collective-permute-start.4) | collective-permute-done | bytes 393248 | tf_op jit(solution)/shard_map/ppermute | solution.py:17
  750.1 6.9 collective-permute-start.5
  758.3 15.5 %collective-permute-done.5 = bf16[256,768]{1,0:T(8,128)(2,1)S(1)} collective-permute-done((bf16[256,768]{1,0:T(8,128)(2,1)S(1)}, bf16[256,768]{1,0:T(8,128)(2,1)S(1)}, u32[]{:S(2)}, u32[]{:S(2)}) %collective-permute-start.5) | collective-permute-done | bytes 393248 | tf_op jit(solution)/shard_map/ppermute | solution.py:17
  (53 shorter events, 36.2 us)
Async XLA Ops:
  7.2 518.1 %copy-start = (bf16[1,256,768]{2,1,0:T(8,128)(2,1)S(1)}, bf16[1,256,768]{2,1,0:T(8,128)(2,1)}, u32[]{:S(2)}) copy-start(bf16[1,256,768]{2,1,0:T(8,128)(2,1)} %param.11) | copy-start | bytes 1179652
  7.2 20.5 %copy-start.7 = (s32[1,128]{1,0:T(1,128)S(1)}, s32[1,128]{1,0:T(1,128)}, u32[]{:S(2)}) copy-start(s32[1,128]{1,0:T(1,128)} %param.15) | copy-start | bytes 1540
  7.2 182.7 %all-gather.6.cloned.1.call-start = ((), (), s32[]{:S(2)}) async-start(), calls=%async_computation.4 | async-start | bytes 4456448 | tf_op jit(solution)/shard_map/all_gather | solution.py:68
  10.2 78.3 %all-to-all-start = ((bf16[16,128,256]{2,1,0:T(8,128)(2,1)}), bf16[16,128,256]{2,1,0:T(8,128)(2,1)S(1)}, u32[]{:S(2)}, u32[]{:S(2)}) async-start(bf16[16,128,256]{2,1,0:T(8,128)(2,1)} %stack.2), calls=%async_computation | async-start | bytes 2097152 | tf_op jit(solution)/shard_map/all_to_all | solution.py:60
  27.6 385.8 %all-reduce.3.cloned.1.call-start = ((), (), s32[]{:S(2)}) async-start(), calls=%async_computation.5 | async-start | bytes 2097152 | tf_op jit(solution)/shard_map/psum | solution.py:95
  88.6 101.3 %copy-start.1 = (bf16[1,128,4096]{2,1,0:T(8,128)(2,1)S(1)}, bf16[1,128,4096]{2,1,0:T(8,128)(2,1)}, u32[]{:S(2)}) copy-start(bf16[1,128,4096]{2,1,0:T(8,128)(2,1)} %param.10) | copy-start | bytes 3145732
  189.9 6.6 copy-start.8
  208.4 311.9 %all-gather.4.cloned.1.call-start = ((), (), s32[]{:S(2)}) async-start(), calls=%async_computation.3 | async-start | bytes 2228224 | tf_op jit(solution)/shard_map/all_gather | solution.py:100
  529.5 14.0 %copy-start.6 = (f32[1,4096]{1,0:T(1,128)S(1)}, f32[1,4096]{1,0:T(1,128)}, u32[]{:S(2)}) copy-start(f32[1,4096]{1,0:T(1,128)} %param.13) | copy-start | bytes 49156
  529.5 90.8 %all-to-all-start.1 = ((f32[16,128,256]{2,1,0:T(8,128)}), f32[16,128,256]{2,1,0:T(8,128)S(1)}, u32[]{:S(2)}, u32[]{:S(2)}) async-start(f32[16,128,256]{2,1,0:T(8,128)} %fusion.43), calls=%async_computation.1 | async-start | bytes 4194304 | tf_op jit(solution)/shard_map/all_to_all | solution.py:104
  620.3 74.6 %copy-start.2 = (bf16[2048,512]{0,1:T(8,128)(2,1)S(1)}, bf16[2048,512]{0,1:T(8,128)(2,1)}, u32[]{:S(2)}) copy-start(bf16[2048,512]{0,1:T(8,128)(2,1)} %all-gather.4.cloned.1.call-done) | copy-start | bytes 6291460
  620.3 74.6 %copy-start.3 = (bf16[2048,128]{0,1:T(8,128)(2,1)S(1)}, bf16[2048,128]{0,1:T(8,128)(2,1)}, u32[]{:S(2)}) copy-start(bf16[2048,128]{0,1:T(8,128)(2,1)} %copy.29) | copy-start | bytes 1572868
  620.3 74.6 %copy-start.4 = (bf16[2048,128]{0,1:T(8,128)(2,1)S(1)}, bf16[2048,128]{0,1:T(8,128)(2,1)}, u32[]{:S(2)}) copy-start(bf16[2048,128]{0,1:T(8,128)(2,1)} %copy.30) | copy-start | bytes 1572868
  696.0 5.7 collective-permute-start.1
  701.7 15.0 %collective-permute-start.2 = (bf16[256,768]{1,0:T(8,128)(2,1)}, bf16[256,768]{1,0:T(8,128)(2,1)}, u32[]{:S(2)}, u32[]{:S(2)}) collective-permute-start(bf16[256,768]{1,0:T(8,128)(2,1)} %collective-permute-done.1), channel_id=1, source_target_pairs={{0,32},{16,48},{32,0},{48,16},{64,96},{80,112},{96,64},{112,80},{1... | collective-permute-start | bytes 1179656 | tf_op jit(solution)/shard_map/ppermute | solution.py:17
  711.3 62.5 %copy-start.5 = (bf16[1,256,768]{2,1,0:T(8,128)(2,1)S(1)}, bf16[1,256,768]{2,1,0:T(8,128)(2,1)}, u32[]{:S(2)}) copy-start(bf16[1,256,768]{2,1,0:T(8,128)(2,1)} %param.14) | copy-start | bytes 1179652
  716.7 15.4 %collective-permute-start.3 = (bf16[256,768]{1,0:T(8,128)(2,1)}, bf16[256,768]{1,0:T(8,128)(2,1)S(1)}, u32[]{:S(2)}, u32[]{:S(2)}) collective-permute-start(bf16[256,768]{1,0:T(8,128)(2,1)} %collective-permute-done.2), channel_id=1, source_target_pairs={{0,64},{16,80},{32,96},{48,112},{64,0},{80,16},{96,32},{112,48},{1... | collective-permute-start | bytes 1179656 | tf_op jit(solution)/shard_map/ppermute | solution.py:17
  726.0 31.0 %collective-permute-start = (bf16[128,4096]{0,1:T(8,128)(2,1)S(1)}, bf16[128,4096]{0,1:T(8,128)(2,1)S(1)}, u32[]{:S(2)}, u32[]{:S(2)}) collective-permute-start(bf16[128,4096]{0,1:T(8,128)(2,1)S(1)} %fusion.18), channel_id=1, source_target_pairs={{0,16},{16,32},{32,48},{48,64},{64,80},{80,96},{96,112},{112,128},... | collective-permute-start | bytes 3145736 | tf_op jit(solution)/shard_map/ppermute | solution.py:13
  732.1 18.0 %collective-permute-start.4 = (bf16[256,768]{1,0:T(8,128)(2,1)S(1)}, bf16[256,768]{1,0:T(8,128)(2,1)S(1)}, u32[]{:S(2)}, u32[]{:S(2)}) collective-permute-start(bf16[256,768]{1,0:T(8,128)(2,1)S(1)} %collective-permute-done.3), channel_id=1, source_target_pairs={{0,128},{16,144},{32,160},{48,176},{64,192},{80,208},{96,224},{112... | collective-permute-start | bytes 1179656 | tf_op jit(solution)/shard_map/ppermute | solution.py:17
  750.1 23.7 %collective-permute-start.5 = (bf16[256,768]{1,0:T(8,128)(2,1)S(1)}, bf16[256,768]{1,0:T(8,128)(2,1)S(1)}, u32[]{:S(2)}, u32[]{:S(2)}) collective-permute-start(bf16[256,768]{1,0:T(8,128)(2,1)S(1)} %collective-permute-done.4), channel_id=1, source_target_pairs={{0,256},{16,272},{32,288},{48,304},{64,320},{80,336},{96,352},{112... | collective-permute-start | bytes 1179656 | tf_op jit(solution)/shard_map/ppermute | solution.py:17
Sparse Core Ops, SparseCore 0:
  11.0 178.8 all-gather.5
  208.6 204.7 all-reduce.2
  417.4 102.9 all-gather.3
